TPU v7x, 128 devices: a whole 4x4x4 slice. The times are simulated.
128 devices in a mesh: region: 8 (over x, core), unit: 16 (over y, z).
Axes of the slice: x: 4, y: 4, z: 4, core: 2. Of those that a mesh axis runs over, the one named last changes fastest.
Arguments:
- noisy: bfloat16 [32768, 2048], P(('region', 'unit')), may hold values from -6 to 6
- strategy: bfloat16 [2048, 2048], replicated, may hold values from -0.125 to 0.125
- county_hist: float32 [1024, 2048], P(('region', 'unit')), may hold values from -24 to 24
- tract_county: int32 [32768], P(('region', 'unit')), may hold values from 0 to 1023, as said below
- tract_owner: int32 [32768, 1], P(('region', 'unit')), may hold values from 0 to 127; in each aligned block of 256 rows (0 to 255, 256 to 511, ...) at most 4 rows name the same one
Outputs:
- released: bfloat16 [32768, 2048], P(('region', 'unit'))
- relaid: float32 [65536, 2048], P(('region', 'unit'))
Inputs may be any that keep to these rules, and one draw needn't show every extreme that they name: `tract_county`: every county has at least one tract; the tracts of region r (rows r * 256 * 16 onward) lie in counties of region r (rows r * 8 * 16 onward of county_hist). `tract_owner`: among the 256 rows of one device no owner appears more than 4 times, and some owner appears exactly 4 times.
All inputs are finite; a program needn't handle non-finite values.
Results may differ from a plain program's by a relative error of at most 0.005.
Values sent between devices are 32-bit elements; how exact they have to be, the bound alone decides.
No kernel may reach another device: no remote copies, remote signals or barrier semaphores. Data moves between devices by JAX's collectives and lax.ppermute only.
A program may use at most 64 MiB of HBM per device.

v0:
```python
import jax
import jax.numpy as jnp
from jax import lax
from jax.sharding import PartitionSpec as P

ITERS = 2
step_size = 0.25


def local(noisy, strategy, county_hist, tract_county, tract_owner):
    unit_count = lax.axis_size("unit")
    region_count = lax.axis_size("region")
    devices = region_count * unit_count
    tract_rows = noisy.shape[0]
    width = strategy.shape[0]
    county_region = county_hist.shape[0] * unit_count
    first_county = lax.axis_index("region") * county_region
    local_id = tract_county - first_county
    member = (local_id[:, None] == jnp.arange(county_region, dtype=jnp.int32)[None, :]).astype(
        jnp.float32
    )
    county_tally = jnp.sum(member, axis=0)
    estimate = jnp.zeros((tract_rows, width), jnp.float32)
    for iteration in range(ITERS):
        if iteration == 0:
            misfit = -noisy
        else:
            answers = jnp.dot(
                estimate.astype(jnp.bfloat16), strategy, preferred_element_type=jnp.float32
            )
            misfit = (answers - noisy.astype(jnp.float32)).astype(jnp.bfloat16)
        gradient = lax.dot_general(
            misfit, strategy, (((1,), (1,)), ((), ())), preferred_element_type=jnp.float32
        )
        stepped = estimate - step_size * gradient
        partial_value = lax.dot_general(
            member,
            stepped,
            (((0,), (0,)), ((), ())),
            precision=lax.Precision.HIGHEST,
            preferred_element_type=jnp.float32,
        )
        child_total, tract_count = (
            lax.psum_scatter(partial_value, "unit", scatter_dimension=0, tiled=True),
            lax.psum_scatter(county_tally, "unit", scatter_dimension=0, tiled=True),
        )
        parent_gap = (county_hist - child_total) / tract_count[:, None]
        region_gap = lax.all_gather(parent_gap, "unit", axis=0, tiled=True)
        estimate = stepped + jnp.dot(
            member, region_gap, precision=lax.Precision.HIGHEST, preferred_element_type=jnp.float32
        )
    owners = tract_owner[:, 0]
    owner_hits = (owners[:, None] == jnp.arange(devices, dtype=jnp.int32)[None, :]).astype(
        jnp.int32
    )
    slot_index = jnp.sum((jnp.cumsum(owner_hits, axis=0) - owner_hits) * owner_hits, axis=1)
    capacity = 2 * tract_rows // devices
    target = owners * capacity + slot_index
    outgoing = jnp.zeros((devices * capacity, width), jnp.float32).at[target].set(estimate)
    released = jnp.dot(
        estimate.astype(jnp.bfloat16), strategy, preferred_element_type=jnp.float32
    ).astype(jnp.bfloat16)
    grouped = outgoing.reshape(devices, capacity, width)
    arrived = lax.all_to_all(grouped, ("region", "unit"), split_axis=0, concat_axis=0, tiled=True)
    relaid = arrived.reshape(devices * capacity, width)
    return (released, relaid)


def solution(mesh):
    in_specs = (
        P(("region", "unit"), None),
        P(),
        P(("region", "unit"), None),
        P(("region", "unit")),
        P(("region", "unit"), None),
    )
    out_specs = (P(("region", "unit"), None), P(("region", "unit"), None))
    return jax.shard_map(local, mesh=mesh, in_specs=in_specs, out_specs=out_specs, check_vma=False)
```

profile of v0, /device:TPU:6, one launch (start us, length us, event | category | flops | bytes accessed | tf_op | source)
XLA Modules:
  0.0 385.6 jit_solution(13782813712799772541)
XLA Ops:
  7.2 0.0 all-reduce.6.cloned.1.call-start
  7.2 0.7 broadcast_subtract_fusion
  7.9 6.1 %fusion = f32[256,2048]{1,0:T(8,128)S(1)} fusion(bf16[2048,2048]{1,0:T(8,128)(2,1)} %param.6, bf16[256,2048]{1,0:T(8,128)(2,1)} %param.5), kind=kOutput, calls=%fused_computation.5 | convolution fusion | flops 2149056512 | bytes 11534336 | tf_op jit(solution)/shard_map/dot_general | solution.py:32
  14.0 0.0 copy-start.4
  14.0 0.0 copy-start.1
  14.0 1.9 fusion.15
  15.9 0.0 all-reduce.6.cloned.1.call-update
  15.9 0.0 all-gather.3.cloned.1.call-start
  16.0 0.0 copy-done.4
  16.0 0.6 dynamic-slice
  17.2 0.1 convert_reduce_fusion
  17.4 42.1 %all-reduce.1 = f32[128]{0:T(128)S(1)} all-reduce(f32[128]{0:T(128)S(1)} %convert_reduce_fusion), channel_id=3, replica_groups=mesh['region'=8,'unit'=16] {'unit'}, use_global_device_ids=true, to_apply=%region_2.0.clone | all-reduce | flops 128 | bytes 1024
  59.4 0.1 dynamic-slice.3
  59.5 46.5 %all-reduce.6.cloned.1.call-done = f32[128,2048]{1,0:T(8,128)} async-done(((f32[128,2048]{1,0:T(8,128)}), f32[128,2048]{1,0:T(8,128)}) %all-reduce.6.cloned.1.call-update) | async-done | bytes 1048592
  106.0 0.0 copy-done.1
  106.0 1.5 fusion.17
  107.5 0.0 all-gather.3.cloned.1.call-update
  107.5 0.0 copy-start.3
  107.5 0.0 all-reduce.8.cloned.1.call-start
  107.6 42.9 %all-gather.3.cloned.1.call-done = f32[128,2048]{1,0:T(8,128)} async-done(((f32[8,2048]{1,0:T(8,128)}), f32[128,2048]{1,0:T(8,128)}) %all-gather.3.cloned.1.call-update) | async-done | bytes 1048592 | tf_op jit(solution)/shard_map/all_gather | solution.py:48
  150.5 3.6 convolution_add_fusion.1
  154.1 0.0 copy-done.3
  154.1 11.5 %fusion.1 = f32[256,2048]{1,0:T(8,128)S(1)} fusion(f32[256,2048]{1,0:T(8,128)} %convolution_add_fusion.1, bf16[2048,2048]{1,0:T(8,128)(2,1)} %param.6, bf16[256,2048]{1,0:T(8,128)(2,1)S(1)} %copy-done.3), kind=kOutput, calls=%fused_computation.6 | convolution fusion | flops 4298113024 | bytes 13631488 | tf_op jit(solution)/shard_map/dot_general | solution.py:32
  165.6 0.0 copy-start.2
  165.6 1.9 fusion.14
  167.5 0.0 all-reduce.8.cloned.1.call-update
  167.5 0.2 all-gather.5.cloned.1.call-start
  167.7 86.7 %all-reduce.8.cloned.1.call-done = f32[128,2048]{1,0:T(8,128)} async-done(((f32[128,2048]{1,0:T(8,128)}), f32[128,2048]{1,0:T(8,128)}) %all-reduce.8.cloned.1.call-update) | async-done | bytes 1048592
  254.4 1.5 fusion.16
  255.9 0.0 all-gather.5.cloned.1.call-update
  256.0 0.0 copy-done.2
  256.0 0.1 copy.12
  256.1 0.2 fusion.10
  256.4 0.2 fusion.12
  256.6 42.2 %all-gather.5.cloned.1.call-done = f32[128,2048]{1,0:T(8,128)} async-done(((f32[8,2048]{1,0:T(8,128)}), f32[128,2048]{1,0:T(8,128)}) %all-gather.5.cloned.1.call-update) | async-done | bytes 1048592 | tf_op jit(solution)/shard_map/all_gather | solution.py:48
  298.8 3.6 convolution_add_fusion
  302.4 5.1 %scatter_custom_fusion = f32[512,2048]{1,0:T(8,128)} fusion(s32[256]{0:T(256)S(1)} %bitcast.33, f32[256,2048]{1,0:T(8,128)} %convolution_add_fusion, f32[]{:T(128)} %constant.8.clone.1), kind=kCustom, calls=%fused_computation.10 | custom fusion | bytes 4194816 | tf_op jit(solution)/shard_map/scatter | solution.py:59
  307.6 5.2 %reshape.30 = f32[128,4,2048]{2,1,0:T(4,128)} reshape(f32[512,2048]{1,0:T(8,128)} %scatter_custom_fusion) | data formatting | bytes 8388608 | tf_op jit(solution)/shard_map/reshape | solution.py:63
  312.7 0.0 copy-start
  312.7 7.8 %all-to-all-start = ((f32[128,4,2048]{2,1,0:T(4,128)}), f32[128,4,2048]{2,1,0:T(4,128)}, u32[]{:S(2)}, u32[]{:S(2)}) async-start(f32[128,4,2048]{2,1,0:T(4,128)} %reshape.30), calls=%async_computation | async-start | bytes 8388608 | tf_op jit(solution)/shard_map/all_to_all | solution.py:64
  320.6 0.0 copy-done
  320.6 6.7 %convolution_convert_fusion = bf16[256,2048]{1,0:T(8,128)(2,1)} fusion(bf16[2048,2048]{1,0:T(8,128)(2,1)} %param.6, f32[256,2048]{1,0:T(8,128)S(1)} %copy-done), kind=kOutput, calls=%fused_computation.9 | convolution fusion | flops 2148532224 | bytes 11534336 | tf_op jit(solution)/shard_map/dot_general | solution.py:60
  327.3 46.5 %all-to-all-done = f32[128,4,2048]{2,1,0:T(4,128)} async-done(((f32[128,4,2048]{2,1,0:T(4,128)}), f32[128,4,2048]{2,1,0:T(4,128)}, u32[]{:S(2)}, u32[]{:S(2)}) %all-to-all-start) | async-done | bytes 4194336 | tf_op jit(solution)/shard_map/all_to_all | solution.py:64
  373.8 5.3 %reshape.31 = f32[512,2048]{1,0:T(8,128)} reshape(f32[128,4,2048]{2,1,0:T(4,128)} %all-to-all-done) | data formatting | bytes 8388608 | tf_op jit(solution)/shard_map/reshape | solution.py:65
  (7 shorter events, 0.1 us)
Async XLA Ops:
  7.2 98.8 %all-reduce.6.cloned.1.call-start = ((), (), s32[]{:S(2)}) async-start(), calls=%async_computation.3 | async-start | bytes 2097152
  14.0 2.0 copy-start.4
  14.0 92.0 %copy-start.1 = (f32[8,2048]{1,0:T(8,128)S(1)}, f32[8,2048]{1,0:T(8,128)}, u32[]{:S(2)}) copy-start(f32[8,2048]{1,0:T(8,128)} %param.7) | copy-start | bytes 196612
  15.9 134.5 %all-gather.3.cloned.1.call-start = ((), (), s32[]{:S(2)}) async-start(), calls=%async_computation.1 | async-start | bytes 1114112 | tf_op jit(solution)/shard_map/all_gather | solution.py:48
  107.5 46.5 %copy-start.3 = (bf16[256,2048]{1,0:T(8,128)(2,1)S(1)}, bf16[256,2048]{1,0:T(8,128)(2,1)}, u32[]{:S(2)}) copy-start(bf16[256,2048]{1,0:T(8,128)(2,1)} %param.5) | copy-start | bytes 3145732
  107.5 146.9 %all-reduce.8.cloned.1.call-start = ((), (), s32[]{:S(2)}) async-start(), calls=%async_computation.4 | async-start | bytes 2097152
  165.6 90.4 %copy-start.2 = (s32[256,1]{0,1:T(1,128)S(1)}, s32[256,1]{0,1:T(1,128)}, u32[]{:S(2)}) copy-start(s32[256,1]{0,1:T(1,128)} %param.9) | copy-start | bytes 3076
  167.5 131.3 %all-gather.5.cloned.1.call-start = ((), (), s32[]{:S(2)}) async-start(), calls=%async_computation.2 | async-start | bytes 1114112 | tf_op jit(solution)/shard_map/all_gather | solution.py:48
  312.7 7.9 %copy-start = (f32[256,2048]{1,0:T(8,128)S(1)}, f32[256,2048]{1,0:T(8,128)}, u32[]{:S(2)}) copy-start(f32[256,2048]{1,0:T(8,128)} %convolution_add_fusion) | copy-start | bytes 6291460
  312.7 61.1 %all-to-all-start = ((f32[128,4,2048]{2,1,0:T(4,128)}), f32[128,4,2048]{2,1,0:T(4,128)}, u32[]{:S(2)}, u32[]{:S(2)}) async-start(f32[128,4,2048]{2,1,0:T(4,128)} %reshape.30), calls=%async_computation | async-start | bytes 8388608 | tf_op jit(solution)/shard_map/all_to_all | solution.py:64
Sparse Core Ops, SparseCore 0:
  16.1 89.8 all-reduce.5
  108.7 41.7 all-gather.2
  167.6 86.7 all-reduce.7
  257.0 41.7 all-gather.4
where the time goes:
time: 386 us
  waiting for transfers between devices  265 us (69%)
  blocking collectives  42.1 us (11%)
  matrix products  35.3 us (9%)
  local copies, waits for them, and re-layouts  16.4 us (4%)
  between operations  14.5 us (4%)
  starting transfers between devices  8.19 us (2%)
  other arithmetic  4.33 us (1%)
    unnamed x6, waiting for transfers between devices  133 us
    all_gather x2, waiting for transfers between devices, local(): region_gap = lax.all_gather(parent_gap, 'unit', axis=0, tiled=True)  85.1 us
    all_to_all x1, waiting for transfers between devices, local(): lax.all_to_all(grouped, ('region', 'unit'), split_axis=0, concat_axis=0,...  46.5 us
    unnamed x1, blocking collectives  42.1 us
    dot_general x2, matrix products, local(): lax.dot_general(misfit, strategy, (((1,), (1,)), ((), ())), preferred_ele...  17.6 us
    all_to_all x1, starting transfers between devices, local(): lax.all_to_all(grouped, ('region', 'unit'), split_axis=0, concat_axis=0,...  7.85 us
  transfers between devices with their start and end apart: 5, of which 5 were waited for; matrix products, arithmetic and copies ran while one was open for 2% of the time, Pallas kernels for 0%

commit v1 on v0

--- a/solution.py
+++ b/solution.py
@@ -1,3 +1,4 @@
+import functools
 import jax
 import jax.numpy as jnp
 from jax import lax
@@ -5,6 +6,21 @@
 
 ITERS = 2
 step_size = 0.25
+
+
+def get_the_map(local_block, net_axis, array_axis):
+    num = lax.psum(1, axis_name=net_axis)
+    history = list(map(lambda k: num if k == array_axis else 1, range(local_block.ndim)))
+    return lax.all_to_all(
+        jnp.tile(local_block, history),
+        split_axis=array_axis,
+        tiled=True,
+        axis_name=net_axis,
+        concat_axis=array_axis,
+    )
+
+
+_refer_pieces_all = functools.partial(get_the_map, net_axis="unit", array_axis=0)
 
 
 def local(noisy, strategy, county_hist, tract_county, tract_owner):
@@ -45,7 +61,7 @@
             lax.psum_scatter(county_tally, "unit", scatter_dimension=0, tiled=True),
         )
         parent_gap = (county_hist - child_total) / tract_count[:, None]
-        region_gap = lax.all_gather(parent_gap, "unit", axis=0, tiled=True)
+        region_gap = _refer_pieces_all(parent_gap)
         estimate = stepped + jnp.dot(
             member, region_gap, precision=lax.Precision.HIGHEST, preferred_element_type=jnp.float32
         )

time: 386 us -> 335 us (0.87)
  waiting for transfers between devices: 265 us -> 193 us
  blocking collectives: 42.1 us -> 61.8 us
    all_gather x2 -> x0, waiting for transfers between devices: 85.1 us -> none  [local(): region_gap = lax.all_gather(parent_gap, 'unit', axis=0, tiled=True)]
    all_to_all x0 -> x1, blocking collectives: none -> 19.8 us  [get_the_map(): lax.all_to_all(jnp.tile(local_block, history), split_axis=array_axis, til...]
    all_to_all x0 -> x1, waiting for transfers between devices: none -> 14.6 us  [get_the_map(): lax.all_to_all(jnp.tile(local_block, history), split_axis=array_axis, til...]
    all_to_all x0 -> x1, starting transfers between devices: none -> 4.86 us  [get_the_map(): lax.all_to_all(jnp.tile(local_block, history), split_axis=array_axis, til...]
    unnamed x6 -> x4, waiting for transfers between devices: 133 us -> 132 us
  transfers between devices with their start and end apart: 5 -> 4, of which waited for: 5 -> 4; matrix products, arithmetic and copies ran while one was open for 2% -> 2% of each run, Pallas kernels for 0% -> 0%
where the time goes in v1:
time: 335 us
  waiting for transfers between devices  193 us (58%)
  blocking collectives  61.8 us (18%)
  matrix products  32.9 us (10%)
  local copies, waits for them, and re-layouts  17.6 us (5%)
  between operations  14.8 us (4%)
  starting transfers between devices  11.4 us (3%)
    unnamed x4, waiting for transfers between devices  132 us
    all_to_all x1, waiting for transfers between devices, local(): lax.all_to_all(grouped, ('region', 'unit'), split_axis=0, concat_axis=0,...  46.5 us
    unnamed x1, blocking collectives  42.1 us
    all_to_all x1, blocking collectives, get_the_map(): lax.all_to_all(jnp.tile(local_block, history), split_axis=array_axis, til...  19.8 us
    dot_general x2, matrix products, local(): lax.dot_general(misfit, strategy, (((1,), (1,)), ((), ())), preferred_ele...  17.6 us
    all_to_all x1, waiting for transfers between devices, get_the_map(): lax.all_to_all(jnp.tile(local_block, history), split_axis=array_axis, til...  14.6 us
  transfers between devices with their start and end apart: 4, of which 4 were waited for; matrix products, arithmetic and copies ran while one was open for 2% of the time, Pallas kernels for 0%

profile of v1, /device:TPU:6, one launch (start us, length us, event | category | flops | bytes accessed | tf_op | source)
XLA Modules:
  0.0 334.5 jit_solution(17405523079297468950)
XLA Ops:
  7.2 0.0 all-reduce.6.cloned.1.call-start
  7.2 0.7 broadcast_subtract_fusion
  7.9 6.1 %fusion = f32[256,2048]{1,0:T(8,128)S(1)} fusion(bf16[2048,2048]{1,0:T(8,128)(2,1)} %param.6, bf16[256,2048]{1,0:T(8,128)(2,1)} %param.5), kind=kOutput, calls=%fused_computation.5 | convolution fusion | flops 2149056512 | bytes 11534336 | tf_op jit(solution)/shard_map/dot_general | solution.py:48
  14.0 0.0 copy-start.4
  14.0 0.0 copy-start.1
  14.0 1.9 fusion.17
  15.9 0.0 all-reduce.6.cloned.1.call-update
  15.9 0.0 all-reduce.8.cloned.1.call-start
  16.0 0.0 copy-done.4
  16.0 0.6 dynamic-slice
  17.2 0.1 convert_reduce_fusion
  17.4 42.1 %all-reduce.1 = f32[128]{0:T(128)S(1)} all-reduce(f32[128]{0:T(128)S(1)} %convert_reduce_fusion), channel_id=3, replica_groups=mesh['region'=8,'unit'=16] {'unit'}, use_global_device_ids=true, to_apply=%region_2.0.clone | all-reduce | flops 128 | bytes 1024
  59.4 0.1 dynamic-slice.3
  59.5 46.5 %all-reduce.6.cloned.1.call-done = f32[128,2048]{1,0:T(8,128)} async-done(((f32[128,2048]{1,0:T(8,128)}), f32[128,2048]{1,0:T(8,128)}) %all-reduce.6.cloned.1.call-update) | async-done | bytes 1048592
  106.0 0.0 copy-done.1
  106.0 0.9 fusion.19
  106.9 0.1 tile.4
  107.0 19.8 %all_to_all.23 = f32[16,8,2048]{2,1,0:T(8,128)S(1)} all-to-all(f32[16,8,2048]{2,1,0:T(8,128)S(1)} %tile.4), channel_id=1, replica_groups=mesh['region'=8,'unit'=16] {'unit'}, dimensions={0} | all-to-all | bytes 2097152 | tf_op jit(solution)/shard_map/all_to_all | solution.py:14
  126.7 0.0 copy-start.3
  126.7 2.4 convolution_add_fusion.1
  129.1 0.0 copy-done.3
  129.1 11.5 %fusion.1 = f32[256,2048]{1,0:T(8,128)S(1)} fusion(f32[256,2048]{1,0:T(8,128)} %convolution_add_fusion.1, bf16[2048,2048]{1,0:T(8,128)(2,1)} %param.6, bf16[256,2048]{1,0:T(8,128)(2,1)S(1)} %copy-done.3), kind=kOutput, calls=%fused_computation.6 | convolution fusion | flops 4298113024 | bytes 13631488 | tf_op jit(solution)/shard_map/dot_general | solution.py:48
  140.6 0.0 copy-start.2
  140.6 1.9 fusion.16
  142.5 0.0 all-reduce.8.cloned.1.call-update
  142.6 0.0 copy-done.2
  142.6 0.1 copy.12
  142.7 85.3 %all-reduce.8.cloned.1.call-done = f32[128,2048]{1,0:T(8,128)} async-done(((f32[128,2048]{1,0:T(8,128)}), f32[128,2048]{1,0:T(8,128)}) %all-reduce.8.cloned.1.call-update) | async-done | bytes 1048592
  228.0 0.9 fusion.18
  228.9 1.1 tile.5
  230.0 4.9 %all-to-all-start.1 = ((f32[16,8,2048]{2,1,0:T(8,128)}), f32[16,8,2048]{2,1,0:T(8,128)S(1)}, u32[]{:S(2)}, u32[]{:S(2)}) async-start(f32[16,8,2048]{2,1,0:T(8,128)} %tile.5), calls=%async_computation.1 | async-start | bytes 2097152 | tf_op jit(solution)/shard_map/all_to_all | solution.py:14
  234.8 0.2 fusion.12
  235.1 0.2 fusion.14
  235.3 14.6 %all-to-all-done.1 = f32[16,8,2048]{2,1,0:T(8,128)S(1)} async-done(((f32[16,8,2048]{2,1,0:T(8,128)}), f32[16,8,2048]{2,1,0:T(8,128)S(1)}, u32[]{:S(2)}, u32[]{:S(2)}) %all-to-all-start.1) | async-done | bytes 1048608 | tf_op jit(solution)/shard_map/all_to_all | solution.py:14
  250.0 2.4 convolution_add_fusion
  252.4 5.1 %scatter_custom_fusion = f32[512,2048]{1,0:T(8,128)} fusion(s32[256]{0:T(256)S(1)} %bitcast.37, f32[256,2048]{1,0:T(8,128)} %convolution_add_fusion, f32[]{:T(128)} %constant.8.clone.1), kind=kCustom, calls=%fused_computation.10 | custom fusion | bytes 4194816 | tf_op jit(solution)/shard_map/scatter | solution.py:75
  257.5 5.2 %reshape.44 = f32[128,4,2048]{2,1,0:T(4,128)} reshape(f32[512,2048]{1,0:T(8,128)} %scatter_custom_fusion) | data formatting | bytes 8388608 | tf_op jit(solution)/shard_map/reshape | solution.py:79
  262.7 0.0 copy-start
  262.7 6.5 %all-to-all-start.2 = ((f32[128,4,2048]{2,1,0:T(4,128)}), f32[128,4,2048]{2,1,0:T(4,128)}, u32[]{:S(2)}, u32[]{:S(2)}) async-start(f32[128,4,2048]{2,1,0:T(4,128)} %reshape.44), calls=%async_computation.2 | async-start | bytes 8388608 | tf_op jit(solution)/shard_map/all_to_all | solution.py:80
  269.2 0.0 copy-done
  269.2 6.7 %convolution_convert_fusion = bf16[256,2048]{1,0:T(8,128)(2,1)} fusion(bf16[2048,2048]{1,0:T(8,128)(2,1)} %param.6, f32[256,2048]{1,0:T(8,128)S(1)} %copy-done), kind=kOutput, calls=%fused_computation.9 | convolution fusion | flops 2148532224 | bytes 11534336 | tf_op jit(solution)/shard_map/dot_general | solution.py:76
  275.9 46.5 %all-to-all-done.2 = f32[128,4,2048]{2,1,0:T(4,128)} async-done(((f32[128,4,2048]{2,1,0:T(4,128)}), f32[128,4,2048]{2,1,0:T(4,128)}, u32[]{:S(2)}, u32[]{:S(2)}) %all-to-all-start.2) | async-done | bytes 4194336 | tf_op jit(solution)/shard_map/all_to_all | solution.py:80
  322.4 5.3 %reshape.45 = f32[512,2048]{1,0:T(8,128)} reshape(f32[128,4,2048]{2,1,0:T(4,128)} %all-to-all-done.2) | data formatting | bytes 8388608 | tf_op jit(solution)/shard_map/reshape | solution.py:81
  (7 shorter events, 0.1 us)
Async XLA Ops:
  7.2 98.8 %all-reduce.6.cloned.1.call-start = ((), (), s32[]{:S(2)}) async-start(), calls=%async_computation.3 | async-start | bytes 2097152
  14.0 2.0 copy-start.4
  14.0 92.0 %copy-start.1 = (f32[8,2048]{1,0:T(8,128)S(1)}, f32[8,2048]{1,0:T(8,128)}, u32[]{:S(2)}) copy-start(f32[8,2048]{1,0:T(8,128)} %param.7) | copy-start | bytes 196612
  15.9 212.0 %all-reduce.8.cloned.1.call-start = ((), (), s32[]{:S(2)}) async-start(), calls=%async_computation.4 | async-start | bytes 2097152
  126.7 2.4 copy-start.3
  140.6 1.9 copy-start.2
  230.0 20.0 %all-to-all-start.1 = ((f32[16,8,2048]{2,1,0:T(8,128)}), f32[16,8,2048]{2,1,0:T(8,128)S(1)}, u32[]{:S(2)}, u32[]{:S(2)}) async-start(f32[16,8,2048]{2,1,0:T(8,128)} %tile.5), calls=%async_computation.1 | async-start | bytes 2097152 | tf_op jit(solution)/shard_map/all_to_all | solution.py:14
  262.7 6.5 %copy-start = (f32[256,2048]{1,0:T(8,128)S(1)}, f32[256,2048]{1,0:T(8,128)}, u32[]{:S(2)}) copy-start(f32[256,2048]{1,0:T(8,128)} %convolution_add_fusion) | copy-start | bytes 6291460
  262.7 59.7 %all-to-all-start.2 = ((f32[128,4,2048]{2,1,0:T(4,128)}), f32[128,4,2048]{2,1,0:T(4,128)}, u32[]{:S(2)}, u32[]{:S(2)}) async-start(f32[128,4,2048]{2,1,0:T(4,128)} %reshape.44), calls=%async_computation.2 | async-start | bytes 8388608 | tf_op jit(solution)/shard_map/all_to_all | solution.py:80
Sparse Core Ops, SparseCore 0:
  16.1 89.8 all-reduce.5
  142.7 85.2 all-reduce.7
